TPU v7x, 256 devices: a whole 4x4x8 slice. The times are simulated.
256 devices in a mesh: ctx: 16 (over z, core), tp: 16 (over x, y).
Axes of the slice: x: 4, y: 4, z: 8, core: 2. Of those that a mesh axis runs over, the one named last changes fastest.
Arguments:
- q_act: bfloat16 [64, 128, 4096], P('ctx', None, 'tp'), may hold values from -16 to 16
- k_act: bfloat16 [64, 128, 4096], P('ctx', None, 'tp'), may hold values from -16 to 16
- v_act: bfloat16 [64, 128, 4096], P('ctx', None, 'tp'), may hold values from -6 to 6
- grad_out: bfloat16 [8192, 4096], P(('ctx', 'tp')), may hold values from -24 to 24
- w_out: bfloat16 [4096, 4096], P(None, 'tp'), may hold values from -0.09375 to 0.09375
- nbr_tiles: int32 [64, 12], replicated, may hold values from 0 to 63, as said below
- nbr_valid: int32 [64, 12], replicated, may hold values from 0 to 1, as said below
- slot_of: int32 [64], replicated, may hold values from 0 to 63, as said below
Outputs:
- grad_q: bfloat16 [64, 128, 4096], P('ctx', None, 'tp')
- grad_k: bfloat16 [64, 128, 4096], P('ctx', None, 'tp')
- grad_v: bfloat16 [64, 128, 4096], P('ctx', None, 'tp')
- grad_w_out: bfloat16 [4096, 4096], P('ctx', 'tp')
Inputs may be any that keep to these rules, and one draw needn't show every extreme that they name: `nbr_tiles`: row t lists scenario tiles linked to tile t; the live entries of a row name distinct tiles, one of them t itself. `nbr_valid`: every row has at least one live entry; a tile is named by live entries of at most 12 rows. `slot_of`: a permutation; slots c * 4 to c * 4 + 3 are held by index c of ctx.
All inputs are finite; a program needn't handle non-finite values.
Results may differ from a plain program's by a relative error of at most 0.024.
Values may be sent and summed in bfloat16 or wider, within the bound.
No kernel may reach another device: no remote copies, remote signals or barrier semaphores. Data moves between devices by JAX's collectives and lax.ppermute only.
A program may use at most 128 MiB of HBM per device.

v0:
```python
import math
import jax
import jax.numpy as jnp
from jax import lax
from jax.sharding import PartitionSpec as P

HD = 128


def side_by_side(arrays, axis, dim, along):
    widths = [a.shape[along] for a in arrays]
    both = jnp.concatenate(arrays, axis=along)
    out = lax.all_gather(both, axis, axis=dim, tiled=True)
    return tuple(jnp.split(out, [sum(widths[:k]) for k in range(1, len(widths))], axis=along))


def slot_tables(nbr_tiles, nbr_valid, slot_of):
    tile_count = slot_of.shape[0]
    slot_index = jnp.arange(tile_count, dtype=jnp.int32)
    matches = (slot_of[:, None] == slot_index[None, :]).astype(jnp.int32)
    near_tiles = jnp.einsum("ts,tj->sj", matches, nbr_tiles)
    live_mask = jnp.einsum("ts,tj->sj", matches, nbr_valid)
    found = (near_tiles[:, :, None] == slot_index[None, None, :]).astype(jnp.int32)
    key_slot = jnp.sum(found * slot_of[None, None, :], axis=2)
    return (key_slot, live_mask)


def per_device(q_act, k_act, v_act, grad_out, w_out, nbr_tiles, nbr_valid, slot_of):
    local_tiles, tile_len, col_width = q_act.shape
    head_count = col_width // HD
    score_scale = 1.0 / math.sqrt(HD)
    ctx_count = lax.axis_size("ctx")
    tile_count = local_tiles * ctx_count
    first_slot = lax.axis_index("ctx") * local_tiles
    key_slot, live_mask = slot_tables(nbr_tiles, nbr_valid, slot_of)
    near_slots = lax.dynamic_slice_in_dim(key_slot, first_slot, local_tiles, 0)
    near_live = lax.dynamic_slice_in_dim(live_mask, first_slot, local_tiles, 0)
    list_len = near_slots.shape[1]
    full_rows = lax.all_gather(grad_out, "tp", axis=0, tiled=True)
    grad_flat = jnp.dot(full_rows, w_out, preferred_element_type=jnp.float32).astype(jnp.bfloat16)
    grad_tiles = grad_flat.reshape(local_tiles, tile_len, col_width)
    grad_grid = grad_flat.reshape(local_tiles, tile_len, head_count, HD)
    key_all, value_all = side_by_side((k_act, v_act), "ctx", 0, 1)
    near_keys = key_all[near_slots].reshape(local_tiles, list_len, tile_len, head_count, HD)
    near_values = value_all[near_slots].reshape(local_tiles, list_len, tile_len, head_count, HD)
    query_grid = q_act.reshape(local_tiles, tile_len, head_count, HD)
    live_cells = (near_live > 0)[:, None, None, :, None]
    scores = (
        jnp.einsum("sahd,sjbhd->shajb", query_grid, near_keys, preferred_element_type=jnp.float32)
        * score_scale
    )
    row_peak = jnp.max(jnp.where(live_cells, scores, -1e30), axis=(3, 4), keepdims=True)
    row_total = jnp.sum(
        jnp.where(live_cells, jnp.exp(scores - row_peak), 0.0), axis=(3, 4), keepdims=True
    )
    log_total = row_peak + jnp.log(row_total)
    prob_full = jnp.where(live_cells, jnp.exp(scores - log_total), 0.0)
    prob_half = prob_full.astype(jnp.bfloat16)
    attn_grid = jnp.einsum(
        "shajb,sjbhd->sahd", prob_half, near_values, preferred_element_type=jnp.float32
    ).astype(jnp.bfloat16)
    row_delta = jnp.einsum(
        "sahd,sahd->sha", grad_grid, attn_grid, preferred_element_type=jnp.float32
    )
    grad_prob = jnp.einsum(
        "sahd,sjbhd->shajb", grad_grid, near_values, preferred_element_type=jnp.float32
    )
    grad_score = (prob_full * (grad_prob - row_delta[:, :, :, None, None])).astype(jnp.bfloat16)
    grad_query = (
        jnp.einsum("shajb,sjbhd->sahd", grad_score, near_keys, preferred_element_type=jnp.float32)
        * score_scale
    )
    grad_q = grad_query.astype(jnp.bfloat16).reshape(local_tiles, tile_len, col_width)
    query_all, grad_all = (
        lax.all_gather(q_act, "ctx", axis=0, tiled=True),
        lax.all_gather(grad_tiles, "ctx", axis=0, tiled=True),
    )
    total_all, delta_all = side_by_side((log_total[:, :, :, 0, 0], row_delta), "ctx", 0, 1)
    query_wide = query_all.reshape(tile_count, tile_len, head_count, HD)
    grad_wide = grad_all.reshape(tile_count, tile_len, head_count, HD)
    owned_slots = first_slot + jnp.arange(local_tiles, dtype=jnp.int32)
    pair_hits = (key_slot[:, :, None] == owned_slots[None, None, :]) & (live_mask[:, :, None] > 0)
    named_by = jnp.any(pair_hits, axis=1).astype(jnp.int32)
    rank_of = jnp.cumsum(named_by, axis=0) - 1
    list_pos = jnp.arange(list_len, dtype=jnp.int32)
    placed = (named_by[:, :, None] > 0) & (rank_of[:, :, None] == list_pos[None, None, :])
    slot_index = jnp.arange(tile_count, dtype=jnp.int32)
    picked = jnp.sum(placed.astype(jnp.int32) * slot_index[:, None, None], axis=0)
    picked_live = jnp.any(placed, axis=0)

    def owner_grads(inputs):
        key_tile, value_tile, chosen, chosen_live = inputs
        query_rows = query_wide[chosen]
        grad_rows = grad_wide[chosen]
        total_rows = total_all[chosen]
        delta_rows = delta_all[chosen]
        owner_scores = (
            jnp.einsum("tahd,bhd->thab", query_rows, key_tile, preferred_element_type=jnp.float32)
            * score_scale
        )
        keep_pair = chosen_live[:, None, None, None]
        owner_probs = jnp.where(keep_pair, jnp.exp(owner_scores - total_rows[:, :, :, None]), 0.0)
        owner_grad_prob = jnp.einsum(
            "tahd,bhd->thab", grad_rows, value_tile, preferred_element_type=jnp.float32
        )
        owner_grad_score = (owner_probs * (owner_grad_prob - delta_rows[:, :, :, None])).astype(
            jnp.bfloat16
        )
        grad_key = (
            jnp.einsum(
                "thab,tahd->bhd", owner_grad_score, query_rows, preferred_element_type=jnp.float32
            )
            * score_scale
        )
        grad_value = jnp.einsum(
            "thab,tahd->bhd",
            owner_probs.astype(jnp.bfloat16),
            grad_rows,
            preferred_element_type=jnp.float32,
        )
        return (grad_key.astype(jnp.bfloat16), grad_value.astype(jnp.bfloat16))

    key_local = k_act.reshape(local_tiles, tile_len, head_count, HD)
    value_local = v_act.reshape(local_tiles, tile_len, head_count, HD)
    grad_key_all, grad_value_all = lax.map(
        owner_grads, (key_local, value_local, picked, picked_live)
    )
    grad_k = grad_key_all.reshape(local_tiles, tile_len, col_width)
    grad_v = grad_value_all.reshape(local_tiles, tile_len, col_width)
    attn_flat = attn_grid.reshape(local_tiles * tile_len, col_width)
    grad_weight = lax.psum_scatter(
        lax.dot_general(
            full_rows, attn_flat, (((0,), (0,)), ((), ())), preferred_element_type=jnp.float32
        ).astype(jnp.bfloat16),
        "ctx",
        scatter_dimension=0,
        tiled=True,
    )
    return (grad_q, grad_k, grad_v, grad_weight)


def solution(mesh):
    in_specs = (
        P("ctx", None, "tp"),
        P("ctx", None, "tp"),
        P("ctx", None, "tp"),
        P(("ctx", "tp"), None),
        P(None, "tp"),
        P(),
        P(),
        P(),
    )
    out_specs = (P("ctx", None, "tp"), P("ctx", None, "tp"), P("ctx", None, "tp"), P("ctx", "tp"))
    return jax.shard_map(
        per_device, mesh=mesh, in_specs=in_specs, out_specs=out_specs, check_vma=False
    )
```

profile of v0, /device:TPU:1, one launch (start us, length us, event | category | flops | bytes accessed | tf_op | source)
XLA Modules:
  0.0 342.1 jit_solution(13095757694921598269)
XLA Ops:
  8.7 1.9 pad_maximum_fusion
  10.8 59.7 %all-gather.7.cloned.1.call-done = bf16[512,4096]{1,0:T(8,128)(2,1)} async-done(((bf16[32,4096]{1,0:T(8,128)(2,1)}), bf16[512,4096]{1,0:T(8,128)(2,1)}) %all-gather.7.cloned.1.call-update) | async-done | bytes 4194320 | tf_op jit(solution)/shard_map/all_gather | solution.py:39
  70.5 4.1 %convolution_convert_fusion.1 = bf16[512,256]{1,0:T(8,128)(2,1)} fusion(bf16[512,4096]{1,0:T(8,128)(2,1)} %all-gather.7.cloned.1.call-done, bf16[4096,256]{1,0:T(8,128)(2,1)S(1)} %copy-done), kind=kOutput, calls=%fused_computation.56 | convolution fusion | flops 1073872896 | bytes 6553600 | tf_op jit(solution)/shard_map/dot_general | solution.py:40
  81.3 33.3 %all-gather.9.cloned.1.call-done = bf16[64,128,256]{2,1,0:T(8,128)(2,1)} async-done(((bf16[4,128,256]{2,1,0:T(8,128)(2,1)}), bf16[64,128,256]{2,1,0:T(8,128)(2,1)}) %all-gather.9.cloned.1.call-update) | async-done | bytes 4194320 | tf_op jit(solution)/shard_map/all_gather | solution.py:75
  114.5 6.9 %reshape.119 = bf16[64,128,2,128]{3,2,1,0:T(2,128)(2,1)} reshape(bf16[64,128,256]{2,1,0:T(8,128)(2,1)} %all-gather.9.cloned.1.call-done) | data formatting | bytes 8388608 | tf_op jit(solution)/shard_map/reshape | solution.py:79
  121.5 49.4 %all-gather.5.cloned.1.call-done = bf16[64,256,256]{2,1,0:T(8,128)(2,1)} async-done(((bf16[4,256,256]{2,1,0:T(8,128)(2,1)}), bf16[64,256,256]{2,1,0:T(8,128)(2,1)}) %all-gather.5.cloned.1.call-update) | async-done | bytes 8388624 | tf_op jit(solution)/shard_map/all_gather | solution.py:13
  170.8 6.0 %fusion.65 = (bf16[64,128,256]{2,1,0:T(8,128)(2,1)}, bf16[64,128,256]{2,1,0:T(8,128)(2,1)}) fusion(bf16[64,256,256]{2,1,0:T(8,128)(2,1)} %all-gather.5.cloned.1.call-done), kind=kLoop, calls=%fused_computation.91 | loop fusion | bytes 16777216 | tf_op jit(solution)/shard_map/split | solution.py:14
  176.9 2.9 gather_fusion.4
  179.8 3.0 reshape.114
  182.8 7.2 %copy.136 = bf16[4,12,128,2,128]{2,4,1,3,0:T(8,128)(2,1)S(1)} copy(bf16[4,12,128,2,128]{4,3,2,1,0:T(2,128)(2,1)} %reshape.114) | data formatting | bytes 6291456 | tf_op jit(solution)/shard_map/reshape | solution.py:44
  190.1 4.7 %gather_fusion.5 = bf16[48,128,256]{2,1,0:T(8,128)(2,1)} fusion(bf16[64,128,256]{2,1,0:T(8,128)(2,1)} %get-tuple-element.150, s32[1024]{0:T(1024)S(1)} %pad_clamp_fusion.1), kind=kCustom, calls=%fused_computation.5 | custom fusion | bytes 6291648 | tf_op jit(solution)/shard_map/gather | solution.py:45
  194.8 5.5 %reshape.117 = bf16[4,12,128,2,128]{4,3,2,1,0:T(2,128)(2,1)} reshape(bf16[48,128,256]{2,1,0:T(8,128)(2,1)} %gather_fusion.5) | data formatting | bytes 6291456 | tf_op jit(solution)/shard_map/reshape | solution.py:45
  200.3 8.6 %copy.133 = bf16[4,12,128,2,128]{2,4,1,3,0:T(8,128)(2,1)} copy(bf16[4,12,128,2,128]{4,3,2,1,0:T(2,128)(2,1)} %reshape.117) | data formatting | bytes 6291456 | tf_op jit(solution)/shard_map/reshape | solution.py:45
  209.0 1.9 select_reduce_fusion.1
  215.1 2.4 multiply_reduce_fusion
  217.6 7.6 %fusion.45 = bf16[4,2,128,128]{3,2,1,0:T(8,128)(2,1)} fusion(bf16[4,12,128,2,128]{2,4,1,3,0:T(8,128)(2,1)S(1)} %copy.136, f32[4,2,12,128,128]{4,3,2,1,0:T(8,128)} %copy-done.2, f32[4,2,128]{2,1,0:T(2,128)S(1)} %get-tuple-element.160, f32[4,2,128]{2,1,0:T(2,128)S(1)} %bitcast.194, pred[4,12]{1,0:T(4,128)(4,1)S(1)} %copy.128, ...), kind=kOutput, calls=%fused_computation.55 | convolution fusion | flops 815005696 | bytes 13115440 | tf_op jit(solution)/shard_map/shajb,sjbhd->sahd/dot_general | solution.py:70
  228.0 16.2 %all_gather.18 = f32[64,4,128]{2,1,0:T(4,128)S(1)} all-gather(f32[4,4,128]{2,1,0:T(4,128)S(1)} %pad_maximum_fusion.1), channel_id=1, replica_groups=mesh['ctx'=16,'tp'=16] {'ctx'}, dimensions={0}, use_global_device_ids=true | all-gather | bytes 139264 | tf_op jit(solution)/shard_map/all_gather | solution.py:13
  244.9 4.8 %fusion.27 = bf16[4096,256]{0,1:T(8,128)(2,1)} fusion(bf16[512,4096]{1,0:T(8,128)(2,1)} %all-gather.7.cloned.1.call-done, bf16[64,8,2,128]{3,2,1,0:T(2,128)(2,1)S(1)} %bitcast.185), kind=kOutput, calls=%fused_computation.43 | convolution fusion | flops 1074790400 | bytes 6553600 | tf_op jit(solution)/shard_map/dot_general | solution.py:132
  249.8 7.0 %reshape.123 = bf16[64,128,2,128]{3,2,1,0:T(2,128)(2,1)} reshape(bf16[64,128,256]{2,1,0:T(8,128)(2,1)} %all-gather.11.cloned.1.call-done) | data formatting | bytes 8388608 | tf_op jit(solution)/shard_map/reshape | solution.py:80
  256.7 74.5 %while.12 = (s32[]{:T(128)}, bf16[4,128,2,128]{1,3,2,0:T(8,128)(2,1)S(1)}, bf16[4,128,2,128]{1,3,2,0:T(8,128)(2,1)}, s32[4,12]{1,0:T(4,128)S(1)}, bf16[64,128,2,...) while((s32[]{:T(128)}, ...), condition=%wide.region_8.9_spmd, body=%wide.region_7.8_spmd.sunk | while | flops 405505056 | bytes 14550529 | solution.py:125
  256.8 4.3 %gather_fusion = bf16[12,128,2,128]{3,2,1,0:T(2,128)(2,1)S(1)} fusion(bf16[64,128,2,128]{3,2,1,0:T(2,128)(2,1)} %get-tuple-element.257, s32[1024]{0:T(1024)S(1)} %pad_clamp_fusion.3), kind=kCustom, calls=%fused_computation.clone.1 | custom fusion | bytes 1572912 | tf_op jit(solution)/shard_map/while/body/eval_jaxpr/gather | solution.py:93
  264.6 5.3 %gather_fusion.2 = bf16[12,128,2,128]{3,2,1,0:T(2,128)(2,1)} fusion(bf16[64,128,2,128]{3,2,1,0:T(2,128)(2,1)} %get-tuple-element.262, s32[1024]{0:T(1024)S(1)} %pad_clamp_fusion.3), kind=kCustom, calls=%fused_computation.2.clone.1 | custom fusion | bytes 1572912 | tf_op jit(solution)/shard_map/while/body/eval_jaxpr/gather | solution.py:94
  269.9 2.3 copy.196
  275.4 4.3 %gather_fusion = bf16[12,128,2,128]{3,2,1,0:T(2,128)(2,1)S(1)} fusion(bf16[64,128,2,128]{3,2,1,0:T(2,128)(2,1)} %get-tuple-element.257, s32[1024]{0:T(1024)S(1)} %pad_clamp_fusion.3), kind=kCustom, calls=%fused_computation.clone.1 | custom fusion | bytes 1572912 | tf_op jit(solution)/shard_map/while/body/eval_jaxpr/gather | solution.py:93
  283.2 5.3 %gather_fusion.2 = bf16[12,128,2,128]{3,2,1,0:T(2,128)(2,1)} fusion(bf16[64,128,2,128]{3,2,1,0:T(2,128)(2,1)} %get-tuple-element.262, s32[1024]{0:T(1024)S(1)} %pad_clamp_fusion.3), kind=kCustom, calls=%fused_computation.2.clone.1 | custom fusion | bytes 1572912 | tf_op jit(solution)/shard_map/while/body/eval_jaxpr/gather | solution.py:94
  288.6 2.3 copy.196
  294.0 4.3 %gather_fusion = bf16[12,128,2,128]{3,2,1,0:T(2,128)(2,1)S(1)} fusion(bf16[64,128,2,128]{3,2,1,0:T(2,128)(2,1)} %get-tuple-element.257, s32[1024]{0:T(1024)S(1)} %pad_clamp_fusion.3), kind=kCustom, calls=%fused_computation.clone.1 | custom fusion | bytes 1572912 | tf_op jit(solution)/shard_map/while/body/eval_jaxpr/gather | solution.py:93
  301.8 5.3 %gather_fusion.2 = bf16[12,128,2,128]{3,2,1,0:T(2,128)(2,1)} fusion(bf16[64,128,2,128]{3,2,1,0:T(2,128)(2,1)} %get-tuple-element.262, s32[1024]{0:T(1024)S(1)} %pad_clamp_fusion.3), kind=kCustom, calls=%fused_computation.2.clone.1 | custom fusion | bytes 1572912 | tf_op jit(solution)/shard_map/while/body/eval_jaxpr/gather | solution.py:94
  307.2 2.3 copy.196
  312.6 4.3 %gather_fusion = bf16[12,128,2,128]{3,2,1,0:T(2,128)(2,1)S(1)} fusion(bf16[64,128,2,128]{3,2,1,0:T(2,128)(2,1)} %get-tuple-element.257, s32[1024]{0:T(1024)S(1)} %pad_clamp_fusion.3), kind=kCustom, calls=%fused_computation.clone.1 | custom fusion | bytes 1572912 | tf_op jit(solution)/shard_map/while/body/eval_jaxpr/gather | solution.py:93
  320.5 5.3 %gather_fusion.2 = bf16[12,128,2,128]{3,2,1,0:T(2,128)(2,1)} fusion(bf16[64,128,2,128]{3,2,1,0:T(2,128)(2,1)} %get-tuple-element.262, s32[1024]{0:T(1024)S(1)} %pad_clamp_fusion.3), kind=kCustom, calls=%fused_computation.2.clone.1 | custom fusion | bytes 1572912 | tf_op jit(solution)/shard_map/while/body/eval_jaxpr/gather | solution.py:94
  325.8 2.3 copy.196
  (121 shorter events, 46.7 us)
Async XLA Ops:
  7.2 63.3 %copy-start = (bf16[4096,256]{1,0:T(8,128)(2,1)S(1)}, bf16[4096,256]{1,0:T(8,128)(2,1)}, u32[]{:S(2)}) copy-start(bf16[4096,256]{1,0:T(8,128)(2,1)} %param.14) | copy-start | bytes 6291460
  7.2 63.3 %all-gather.7.cloned.1.call-start = ((), (), s32[]{:S(2)}) async-start(), calls=%async_computation.2 | async-start | bytes 4456448 | tf_op jit(solution)/shard_map/all_gather | solution.py:39
  7.9 106.6 %all-gather.9.cloned.1.call-start = ((), (), s32[]{:S(2)}) async-start(), calls=%async_computation.3 | async-start | bytes 4456448 | tf_op jit(solution)/shard_map/all_gather | solution.py:75
  8.7 162.2 %all-gather.5.cloned.1.call-start = ((), (), s32[]{:S(2)}) async-start(), calls=%async_computation.1 | async-start | bytes 8912896 | tf_op jit(solution)/shard_map/all_gather | solution.py:13
  10.6 64.1 %copy-start.6 = (bf16[4,128,256]{2,1,0:T(8,128)(2,1)S(1)}, bf16[4,128,256]{2,1,0:T(8,128)(2,1)}, u32[]{:S(2)}) copy-start(bf16[4,128,256]{2,1,0:T(8,128)(2,1)} %param.10) | copy-start | bytes 786436
  10.7 64.2 %copy-start.7 = (bf16[4,128,256]{2,1,0:T(8,128)(2,1)S(1)}, bf16[4,128,256]{2,1,0:T(8,128)(2,1)}, u32[]{:S(2)}) copy-start(bf16[4,128,256]{2,1,0:T(8,128)(2,1)} %param.11) | copy-start | bytes 786436
  10.7 65.0 %copy-start.8 = (bf16[4,128,256]{2,1,0:T(8,128)(2,1)S(1)}, bf16[4,128,256]{2,1,0:T(8,128)(2,1)}, u32[]{:S(2)}) copy-start(bf16[4,128,256]{2,1,0:T(8,128)(2,1)} %param.12) | copy-start | bytes 786436
  10.7 65.9 %copy-start.11 = (s32[64]{0:T(128)S(1)}, s32[64]{0:T(128)}, u32[]{:S(2)}) copy-start(s32[64]{0:T(128)} %param.17) | copy-start | bytes 772
  10.7 65.9 %copy-start.12 = (s32[64,12]{0,1:T(8,128)S(1)}, s32[64,12]{0,1:T(8,128)}, u32[]{:S(2)}) copy-start(s32[64,12]{0,1:T(8,128)} %param.15) | copy-start | bytes 9220
  10.7 66.7 %copy-start.13 = (s32[64,12]{0,1:T(8,128)S(1)}, s32[64,12]{0,1:T(8,128)}, u32[]{:S(2)}) copy-start(s32[64,12]{0,1:T(8,128)} %param.16) | copy-start | bytes 9220
  10.7 239.1 %all-gather.11.cloned.1.call-start = ((), (), s32[]{:S(2)}) async-start(), calls=%async_computation.4 | async-start | bytes 4456448 | tf_op jit(solution)/shard_map/all_gather | solution.py:76
  74.7 259.2 %reduce-scatter.2.cloned.1.call-start = ((), (), s32[]{:S(2)}) async-start(), calls=%async_computation.5 | async-start | bytes 2228224 | tf_op jit(solution)/shard_map/reduce_scatter | solution.py:131
  80.1 41.4 %copy-start.4 = (bf16[4,128,2,128]{3,2,1,0:T(2,128)(2,1)}, bf16[4,128,2,128]{3,2,1,0:T(2,128)(2,1)S(1)}, u32[]{:S(2)}) copy-start(bf16[4,128,2,128]{3,2,1,0:T(2,128)(2,1)S(1)} %reshape.116) | copy-start | bytes 786436
  210.9 3.2 copy-start.2
  210.9 4.2 %copy-start.3 = (bf16[4,12,128,2,128]{2,4,1,3,0:T(8,128)(2,1)S(1)}, bf16[4,12,128,2,128]{2,4,1,3,0:T(8,128)(2,1)}, u32[]{:S(2)}) copy-start(bf16[4,12,128,2,128]{2,4,1,3,0:T(8,128)(2,1)} %copy.133) | copy-start | bytes 9437188
  210.9 4.2 %copy-start.9 = (f32[4,2,128,128]{2,3,1,0:T(8,128)S(1)}, f32[4,2,128,128]{2,3,1,0:T(8,128)}, u32[]{:S(2)}) copy-start(f32[4,2,128,128]{2,3,1,0:T(8,128)} %copy.167) | copy-start | bytes 1572868
  215.1 2.4 copy-start.5
  249.7 7.0 %copy-start.10 = (bf16[4,128,2,128]{1,3,2,0:T(8,128)(2,1)S(1)}, bf16[4,128,2,128]{1,3,2,0:T(8,128)(2,1)}, u32[]{:S(2)}) copy-start(bf16[4,128,2,128]{1,3,2,0:T(8,128)(2,1)} %custom-call.12) | copy-start | bytes 786436
  331.2 4.3 %copy-start.1 = (bf16[4096,256]{1,0:T(8,128)(2,1)S(1)}, bf16[4096,256]{1,0:T(8,128)(2,1)}, u32[]{:S(2)}) copy-start(bf16[4096,256]{1,0:T(8,128)(2,1)} %param.14) | copy-start | bytes 6291460
Sparse Core Ops, SparseCore 0:
  10.4 60.0 all-gather.6
  72.3 42.1 all-gather.8
  116.4 54.3 all-gather.4
  173.1 40.4 all-gather.10
  249.9 56.4 reduce-scatter.1
where the time goes:
time: 344 us; the launch traced here: 342 us
  waiting for transfers between devices  144 us (42%)
  local copies, waits for them, and re-layouts  126 us (37%)
  matrix products  36.7 us (11%)
  blocking collectives  16.2 us (5%)
  between operations  14 us (4%)
  other arithmetic  4.96 us (1%)
    all_gather x1, waiting for transfers between devices, per_device(): full_rows = lax.all_gather(grad_out, 'tp', axis=0, tiled=True)  59.7 us
    all_gather x1, waiting for transfers between devices, side_by_side(): out = lax.all_gather(both, axis, axis=dim, tiled=True)  49.4 us
    all_gather x1, waiting for transfers between devices, per_device(): lax.all_gather(q_act, 'ctx', axis=0, tiled=True)  33.3 us
    gather x8, local copies, waits for them, and re-layouts, owner_grads(): grad_rows = grad_wide[chosen]  30.6 us
    gather x8, local copies, waits for them, and re-layouts, owner_grads(): query_rows = query_wide[chosen]  20.1 us
    all_gather x1, blocking collectives, side_by_side(): out = lax.all_gather(both, axis, axis=dim, tiled=True)  16.2 us
    reshape x2, local copies, waits for them, and re-layouts, per_device(): value_all[near_slots]  14.2 us
    reshape x2, local copies, waits for them, and re-layouts, per_device(): key_all[near_slots].reshape(local_tiles, list_len, tile_len, head_count, HD)  10.3 us
  transfers between devices with their start and end apart: 5, of which 3 were waited for; matrix products, arithmetic and copies ran while one was open for 48% of the time, Pallas kernels for 0%

commit v1 on v0

--- a/solution.py
+++ b/solution.py
@@ -5,6 +5,12 @@
 from jax.sharding import PartitionSpec as P
 
 HD = 128
+
+
+def gather_by_exchange(x, axis, dim):
+    size = lax.axis_size(axis)
+    repeats = [size if d == dim else 1 for d in range(x.ndim)]
+    return lax.all_to_all(jnp.tile(x, repeats), axis, split_axis=dim, concat_axis=dim, tiled=True)
 
 
 def side_by_side(arrays, axis, dim, along):
@@ -72,7 +78,7 @@
     )
     grad_q = grad_query.astype(jnp.bfloat16).reshape(local_tiles, tile_len, col_width)
     query_all, grad_all = (
-        lax.all_gather(q_act, "ctx", axis=0, tiled=True),
+        gather_by_exchange(q_act, "ctx", 0),
         lax.all_gather(grad_tiles, "ctx", axis=0, tiled=True),
     )
     total_all, delta_all = side_by_side((log_total[:, :, :, 0, 0], row_delta), "ctx", 0, 1)

time: 344 us -> 332 us (0.965)
  waiting for transfers between devices: 144 us -> 118 us
  starting transfers between devices: 0.2 us -> 10.1 us
  local copies, waits for them, and re-layouts: 126 us -> 130 us
    all_to_all x0 -> x1, waiting for transfers between devices: none -> 52.1 us  [gather_by_exchange(): lax.all_to_all(jnp.tile(x, repeats), axis, split_axis=dim, concat_axis=di...]
    all_gather x1 -> x0, waiting for transfers between devices: 33.3 us -> none  [per_device(): lax.all_gather(q_act, 'ctx', axis=0, tiled=True)]
    all_gather x1, waiting for transfers between devices: 49.4 us -> 18 us  [side_by_side(): out = lax.all_gather(both, axis, axis=dim, tiled=True)]
    all_gather x1, waiting for transfers between devices: 59.7 us -> 47 us  [per_device(): full_rows = lax.all_gather(grad_out, 'tp', axis=0, tiled=True)]
    all_to_all x0 -> x1, starting transfers between devices: none -> 9.97 us  [gather_by_exchange(): lax.all_to_all(jnp.tile(x, repeats), axis, split_axis=dim, concat_axis=di...]
  transfers between devices with their start and end apart: 5 -> 5, of which waited for: 3 -> 3; matrix products, arithmetic and copies ran while one was open for 48% -> 51% of each run, Pallas kernels for 0% -> 0%
where the time goes in v1:
time: 332 us; the launch traced here: 330 us
  local copies, waits for them, and re-layouts  130 us (39%)
  waiting for transfers between devices  118 us (36%)
  matrix products  36.7 us (11%)
  blocking collectives  16.2 us (5%)
  between operations  14 us (4%)
  starting transfers between devices  10.1 us (3%)
  other arithmetic  4.96 us (1%)
    all_to_all x1, waiting for transfers between devices, gather_by_exchange(): lax.all_to_all(jnp.tile(x, repeats), axis, split_axis=dim, concat_axis=di...  52.1 us
    all_gather x1, waiting for transfers between devices, per_device(): full_rows = lax.all_gather(grad_out, 'tp', axis=0, tiled=True)  47 us
    gather x8, local copies, waits for them, and re-layouts, owner_grads(): grad_rows = grad_wide[chosen]  30.6 us
    gather x8, local copies, waits for them, and re-layouts, owner_grads(): query_rows = query_wide[chosen]  20.1 us
    all_gather x1, waiting for transfers between devices, side_by_side(): out = lax.all_gather(both, axis, axis=dim, tiled=True)  18 us
    all_gather x1, blocking collectives, side_by_side(): out = lax.all_gather(both, axis, axis=dim, tiled=True)  16.2 us
    reshape x2, local copies, waits for them, and re-layouts, per_device(): value_all[near_slots]  14.3 us
    reshape x2, local copies, waits for them, and re-layouts, per_device(): key_all[near_slots].reshape(local_tiles, list_len, tile_len, head_count, HD)  10.3 us
  transfers between devices with their start and end apart: 5, of which 3 were waited for; matrix products, arithmetic and copies ran while one was open for 51% of the time, Pallas kernels for 0%

profile of v1, /device:TPU:1, one launch (start us, length us, event | category | flops | bytes accessed | tf_op | source)
XLA Modules:
  0.0 329.8 jit_solution(4244768521233593421)
XLA Ops:
  9.9 3.4 %tile.4 = bf16[16,4,128,256]{3,2,1,0:T(8,128)(2,1)} broadcast(bf16[4,128,256]{2,1,0:T(8,128)(2,1)} %param.10), dimensions={1,2,3} | broadcast | bytes 4456448 | tf_op jit(solution)/shard_map/tile | solution.py:13
  13.3 10.0 %all-to-all-start = ((bf16[64,128,256]{2,1,0:T(8,128)(2,1)}), bf16[64,128,256]{2,1,0:T(8,128)(2,1)}, u32[]{:S(2)}, u32[]{:S(2)}) async-start(bf16[64,128,256]{2,1,0:T(8,128)(2,1)} %bitcast.182), calls=%async_computation | async-start | bytes 8388608 | tf_op jit(solution)/shard_map/all_to_all | solution.py:13
  23.4 47.0 %all-gather.6.cloned.1.call-done = bf16[512,4096]{1,0:T(8,128)(2,1)} async-done(((bf16[32,4096]{1,0:T(8,128)(2,1)}), bf16[512,4096]{1,0:T(8,128)(2,1)}) %all-gather.6.cloned.1.call-update) | async-done | bytes 4194320 | tf_op jit(solution)/shard_map/all_gather | solution.py:45
  70.4 4.1 %convolution_convert_fusion.1 = bf16[512,256]{1,0:T(8,128)(2,1)} fusion(bf16[512,4096]{1,0:T(8,128)(2,1)} %all-gather.6.cloned.1.call-done, bf16[4096,256]{1,0:T(8,128)(2,1)S(1)} %copy-done), kind=kOutput, calls=%fused_computation.56 | convolution fusion | flops 1073872896 | bytes 6553600 | tf_op jit(solution)/shard_map/dot_general | solution.py:46
  81.2 52.1 %all-to-all-done = bf16[64,128,256]{2,1,0:T(8,128)(2,1)} async-done(((bf16[64,128,256]{2,1,0:T(8,128)(2,1)}), bf16[64,128,256]{2,1,0:T(8,128)(2,1)}, u32[]{:S(2)}, u32[]{:S(2)}) %all-to-all-start) | async-done | bytes 4194336 | tf_op jit(solution)/shard_map/all_to_all | solution.py:13
  133.3 7.0 %reshape.123 = bf16[64,128,2,128]{3,2,1,0:T(2,128)(2,1)} reshape(bf16[64,128,256]{2,1,0:T(8,128)(2,1)} %all-to-all-done) | data formatting | bytes 8388608 | tf_op jit(solution)/shard_map/reshape | solution.py:85
  140.3 18.0 %all-gather.4.cloned.1.call-done = bf16[64,256,256]{2,1,0:T(8,128)(2,1)} async-done(((bf16[4,256,256]{2,1,0:T(8,128)(2,1)}), bf16[64,256,256]{2,1,0:T(8,128)(2,1)}) %all-gather.4.cloned.1.call-update) | async-done | bytes 8388624 | tf_op jit(solution)/shard_map/all_gather | solution.py:19
  158.3 6.0 %fusion.65 = (bf16[64,128,256]{2,1,0:T(8,128)(2,1)}, bf16[64,128,256]{2,1,0:T(8,128)(2,1)}) fusion(bf16[64,256,256]{2,1,0:T(8,128)(2,1)} %all-gather.4.cloned.1.call-done), kind=kLoop, calls=%fused_computation.91 | loop fusion | bytes 16777216 | tf_op jit(solution)/shard_map/split | solution.py:20
  164.4 2.9 gather_fusion.4
  167.3 3.0 reshape.118
  170.3 7.3 %copy.136 = bf16[4,12,128,2,128]{2,4,1,3,0:T(8,128)(2,1)S(1)} copy(bf16[4,12,128,2,128]{4,3,2,1,0:T(2,128)(2,1)} %reshape.118) | data formatting | bytes 6291456 | tf_op jit(solution)/shard_map/reshape | solution.py:50
  177.6 4.8 %gather_fusion.5 = bf16[48,128,256]{2,1,0:T(8,128)(2,1)} fusion(bf16[64,128,256]{2,1,0:T(8,128)(2,1)} %get-tuple-element.150, s32[1024]{0:T(1024)S(1)} %pad_clamp_fusion.1), kind=kCustom, calls=%fused_computation.5 | custom fusion | bytes 6291648 | tf_op jit(solution)/shard_map/gather | solution.py:51
  182.4 5.6 %reshape.121 = bf16[4,12,128,2,128]{4,3,2,1,0:T(2,128)(2,1)} reshape(bf16[48,128,256]{2,1,0:T(8,128)(2,1)} %gather_fusion.5) | data formatting | bytes 6291456 | tf_op jit(solution)/shard_map/reshape | solution.py:51
  188.0 8.7 %copy.133 = bf16[4,12,128,2,128]{2,4,1,3,0:T(8,128)(2,1)} copy(bf16[4,12,128,2,128]{4,3,2,1,0:T(2,128)(2,1)} %reshape.121) | data formatting | bytes 6291456 | tf_op jit(solution)/shard_map/reshape | solution.py:51
  202.8 2.4 multiply_reduce_fusion
  205.2 7.6 %fusion.45 = bf16[4,2,128,128]{3,2,1,0:T(8,128)(2,1)} fusion(bf16[4,12,128,2,128]{2,4,1,3,0:T(8,128)(2,1)S(1)} %copy.136, f32[4,2,12,128,128]{4,3,2,1,0:T(8,128)} %copy-done.2, f32[4,2,128]{2,1,0:T(2,128)S(1)} %get-tuple-element.160, f32[4,2,128]{2,1,0:T(2,128)S(1)} %bitcast.196, pred[4,12]{1,0:T(4,128)(4,1)S(1)} %copy.128, ...), kind=kOutput, calls=%fused_computation.55 | convolution fusion | flops 815005696 | bytes 13115440 | tf_op jit(solution)/shard_map/shajb,sjbhd->sahd/dot_general | solution.py:76
  215.7 16.2 %all_gather.14 = f32[64,4,128]{2,1,0:T(4,128)S(1)} all-gather(f32[4,4,128]{2,1,0:T(4,128)S(1)} %pad_maximum_fusion.1), channel_id=1, replica_groups=mesh['ctx'=16,'tp'=16] {'ctx'}, dimensions={0}, use_global_device_ids=true | all-gather | bytes 139264 | tf_op jit(solution)/shard_map/all_gather | solution.py:19
  232.6 4.8 %fusion.27 = bf16[4096,256]{0,1:T(8,128)(2,1)} fusion(bf16[512,4096]{1,0:T(8,128)(2,1)} %all-gather.6.cloned.1.call-done, bf16[64,8,2,128]{3,2,1,0:T(2,128)(2,1)S(1)} %bitcast.187), kind=kOutput, calls=%fused_computation.43 | convolution fusion | flops 1074790400 | bytes 6553600 | tf_op jit(solution)/shard_map/dot_general | solution.py:138
  237.4 7.0 %reshape.127 = bf16[64,128,2,128]{3,2,1,0:T(2,128)(2,1)} reshape(bf16[64,128,256]{2,1,0:T(8,128)(2,1)} %all-gather.8.cloned.1.call-done) | data formatting | bytes 8388608 | tf_op jit(solution)/shard_map/reshape | solution.py:86
  244.4 74.5 %while.12 = (s32[]{:T(128)}, bf16[4,128,2,128]{1,3,2,0:T(8,128)(2,1)S(1)}, bf16[4,128,2,128]{1,3,2,0:T(8,128)(2,1)}, s32[4,12]{1,0:T(4,128)S(1)}, bf16[64,128,2,...) while((s32[]{:T(128)}, ...), condition=%wide.region_8.9_spmd, body=%wide.region_7.8_spmd.sunk | while | flops 405505056 | bytes 14550529 | solution.py:131
  244.4 4.3 %gather_fusion = bf16[12,128,2,128]{3,2,1,0:T(2,128)(2,1)S(1)} fusion(bf16[64,128,2,128]{3,2,1,0:T(2,128)(2,1)} %get-tuple-element.257, s32[1024]{0:T(1024)S(1)} %pad_clamp_fusion.3), kind=kCustom, calls=%fused_computation.clone.1 | custom fusion | bytes 1572912 | tf_op jit(solution)/shard_map/while/body/eval_jaxpr/gather | solution.py:99
  252.3 5.3 %gather_fusion.2 = bf16[12,128,2,128]{3,2,1,0:T(2,128)(2,1)} fusion(bf16[64,128,2,128]{3,2,1,0:T(2,128)(2,1)} %get-tuple-element.262, s32[1024]{0:T(1024)S(1)} %pad_clamp_fusion.3), kind=kCustom, calls=%fused_computation.2.clone.1 | custom fusion | bytes 1572912 | tf_op jit(solution)/shard_map/while/body/eval_jaxpr/gather | solution.py:100
  257.6 2.3 copy.196
  263.1 4.3 %gather_fusion = bf16[12,128,2,128]{3,2,1,0:T(2,128)(2,1)S(1)} fusion(bf16[64,128,2,128]{3,2,1,0:T(2,128)(2,1)} %get-tuple-element.257, s32[1024]{0:T(1024)S(1)} %pad_clamp_fusion.3), kind=kCustom, calls=%fused_computation.clone.1 | custom fusion | bytes 1572912 | tf_op jit(solution)/shard_map/while/body/eval_jaxpr/gather | solution.py:99
  270.9 5.3 %gather_fusion.2 = bf16[12,128,2,128]{3,2,1,0:T(2,128)(2,1)} fusion(bf16[64,128,2,128]{3,2,1,0:T(2,128)(2,1)} %get-tuple-element.262, s32[1024]{0:T(1024)S(1)} %pad_clamp_fusion.3), kind=kCustom, calls=%fused_computation.2.clone.1 | custom fusion | bytes 1572912 | tf_op jit(solution)/shard_map/while/body/eval_jaxpr/gather | solution.py:100
  276.2 2.3 copy.196
  281.7 4.3 %gather_fusion = bf16[12,128,2,128]{3,2,1,0:T(2,128)(2,1)S(1)} fusion(bf16[64,128,2,128]{3,2,1,0:T(2,128)(2,1)} %get-tuple-element.257, s32[1024]{0:T(1024)S(1)} %pad_clamp_fusion.3), kind=kCustom, calls=%fused_computation.clone.1 | custom fusion | bytes 1572912 | tf_op jit(solution)/shard_map/while/body/eval_jaxpr/gather | solution.py:99
  289.6 5.3 %gather_fusion.2 = bf16[12,128,2,128]{3,2,1,0:T(2,128)(2,1)} fusion(bf16[64,128,2,128]{3,2,1,0:T(2,128)(2,1)} %get-tuple-element.262, s32[1024]{0:T(1024)S(1)} %pad_clamp_fusion.3), kind=kCustom, calls=%fused_computation.2.clone.1 | custom fusion | bytes 1572912 | tf_op jit(solution)/shard_map/while/body/eval_jaxpr/gather | solution.py:100
  294.9 2.3 copy.196
  300.3 4.3 %gather_fusion = bf16[12,128,2,128]{3,2,1,0:T(2,128)(2,1)S(1)} fusion(bf16[64,128,2,128]{3,2,1,0:T(2,128)(2,1)} %get-tuple-element.257, s32[1024]{0:T(1024)S(1)} %pad_clamp_fusion.3), kind=kCustom, calls=%fused_computation.clone.1 | custom fusion | bytes 1572912 | tf_op jit(solution)/shard_map/while/body/eval_jaxpr/gather | solution.py:99
  308.2 5.3 %gather_fusion.2 = bf16[12,128,2,128]{3,2,1,0:T(2,128)(2,1)} fusion(bf16[64,128,2,128]{3,2,1,0:T(2,128)(2,1)} %get-tuple-element.262, s32[1024]{0:T(1024)S(1)} %pad_clamp_fusion.3), kind=kCustom, calls=%fused_computation.2.clone.1 | custom fusion | bytes 1572912 | tf_op jit(solution)/shard_map/while/body/eval_jaxpr/gather | solution.py:100
  313.5 2.3 copy.196
  (121 shorter events, 49.8 us)
Async XLA Ops:
  7.2 63.3 %copy-start = (bf16[4096,256]{1,0:T(8,128)(2,1)S(1)}, bf16[4096,256]{1,0:T(8,128)(2,1)}, u32[]{:S(2)}) copy-start(bf16[4096,256]{1,0:T(8,128)(2,1)} %param.14) | copy-start | bytes 6291460
  7.2 63.2 %all-gather.6.cloned.1.call-start = ((), (), s32[]{:S(2)}) async-start(), calls=%async_computation.3 | async-start | bytes 4456448 | tf_op jit(solution)/shard_map/all_gather | solution.py:45
  7.9 150.4 %all-gather.4.cloned.1.call-start = ((), (), s32[]{:S(2)}) async-start(), calls=%async_computation.2 | async-start | bytes 8912896 | tf_op jit(solution)/shard_map/all_gather | solution.py:19
  13.3 120.0 %all-to-all-start = ((bf16[64,128,256]{2,1,0:T(8,128)(2,1)}), bf16[64,128,256]{2,1,0:T(8,128)(2,1)}, u32[]{:S(2)}, u32[]{:S(2)}) async-start(bf16[64,128,256]{2,1,0:T(8,128)(2,1)} %bitcast.182), calls=%async_computation | async-start | bytes 8388608 | tf_op jit(solution)/shard_map/all_to_all | solution.py:13
  23.3 51.4 %copy-start.4 = (bf16[4,128,256]{2,1,0:T(8,128)(2,1)S(1)}, bf16[4,128,256]{2,1,0:T(8,128)(2,1)}, u32[]{:S(2)}) copy-start(bf16[4,128,256]{2,1,0:T(8,128)(2,1)} %param.10) | copy-start | bytes 786436
  23.3 51.5 %copy-start.7 = (bf16[4,128,256]{2,1,0:T(8,128)(2,1)S(1)}, bf16[4,128,256]{2,1,0:T(8,128)(2,1)}, u32[]{:S(2)}) copy-start(bf16[4,128,256]{2,1,0:T(8,128)(2,1)} %param.11) | copy-start | bytes 786436
  23.3 52.3 %copy-start.8 = (bf16[4,128,256]{2,1,0:T(8,128)(2,1)S(1)}, bf16[4,128,256]{2,1,0:T(8,128)(2,1)}, u32[]{:S(2)}) copy-start(bf16[4,128,256]{2,1,0:T(8,128)(2,1)} %param.12) | copy-start | bytes 786436
  23.3 53.1 %copy-start.11 = (s32[64]{0:T(128)S(1)}, s32[64]{0:T(128)}, u32[]{:S(2)}) copy-start(s32[64]{0:T(128)} %param.17) | copy-start | bytes 772
  23.3 53.1 %copy-start.12 = (s32[64,12]{0,1:T(8,128)S(1)}, s32[64,12]{0,1:T(8,128)}, u32[]{:S(2)}) copy-start(s32[64,12]{0,1:T(8,128)} %param.15) | copy-start | bytes 9220
  23.3 54.0 %copy-start.13 = (s32[64,12]{0,1:T(8,128)S(1)}, s32[64,12]{0,1:T(8,128)}, u32[]{:S(2)}) copy-start(s32[64,12]{0,1:T(8,128)} %param.16) | copy-start | bytes 9220
  23.3 214.1 %all-gather.8.cloned.1.call-start = ((), (), s32[]{:S(2)}) async-start(), calls=%async_computation.4 | async-start | bytes 4456448 | tf_op jit(solution)/shard_map/all_gather | solution.py:82
  74.6 247.0 %reduce-scatter.2.cloned.1.call-start = ((), (), s32[]{:S(2)}) async-start(), calls=%async_computation.5 | async-start | bytes 2228224 | tf_op jit(solution)/shard_map/reduce_scatter | solution.py:137
  80.0 60.3 %copy-start.5 = (bf16[4,128,2,128]{3,2,1,0:T(2,128)(2,1)}, bf16[4,128,2,128]{3,2,1,0:T(2,128)(2,1)S(1)}, u32[]{:S(2)}) copy-start(bf16[4,128,2,128]{3,2,1,0:T(2,128)(2,1)S(1)} %reshape.120) | copy-start | bytes 786436
  198.6 3.2 copy-start.2
  198.6 4.2 %copy-start.3 = (bf16[4,12,128,2,128]{2,4,1,3,0:T(8,128)(2,1)S(1)}, bf16[4,12,128,2,128]{2,4,1,3,0:T(8,128)(2,1)}, u32[]{:S(2)}) copy-start(bf16[4,12,128,2,128]{2,4,1,3,0:T(8,128)(2,1)} %copy.133) | copy-start | bytes 9437188
  198.6 4.2 %copy-start.9 = (f32[4,2,128,128]{2,3,1,0:T(8,128)S(1)}, f32[4,2,128,128]{2,3,1,0:T(8,128)}, u32[]{:S(2)}) copy-start(f32[4,2,128,128]{2,3,1,0:T(8,128)} %copy.167) | copy-start | bytes 1572868
  202.8 2.4 copy-start.6
  237.4 7.0 %copy-start.10 = (bf16[4,128,2,128]{1,3,2,0:T(8,128)(2,1)S(1)}, bf16[4,128,2,128]{1,3,2,0:T(8,128)(2,1)}, u32[]{:S(2)}) copy-start(bf16[4,128,2,128]{1,3,2,0:T(8,128)(2,1)} %custom-call.12) | copy-start | bytes 786436
  319.0 4.3 %copy-start.1 = (bf16[4096,256]{1,0:T(8,128)(2,1)S(1)}, bf16[4096,256]{1,0:T(8,128)(2,1)}, u32[]{:S(2)}) copy-start(bf16[4096,256]{1,0:T(8,128)(2,1)} %param.14) | copy-start | bytes 6291460
Sparse Core Ops, SparseCore 0:
  10.4 59.9 all-gather.5
  72.2 86.0 all-gather.3
  160.8 40.9 all-gather.7
  237.5 56.6 reduce-scatter.1
